TPU v7x, 512 devices: a whole 4x4x16 slice. The times are simulated.
512 devices in a mesh: ingest: 8 (over y, core), owner: 64 (over x, z).
Axes of the slice: x: 4, y: 4, z: 16, core: 2. Of those that a mesh axis runs over, the one named last changes fastest.
Arguments:
- frame_rows: bfloat16 [2112, 28, 1024], P('owner', None, 'ingest'), may hold values from -32 to 32
- route_owner: int32 [2112], P('owner'), may hold values from 0 to 63, as said below
- route_slot: int32 [2112], P('owner'), may hold values from 0 to 32, as said below
- frames: int32 [2112], P('owner'), may hold values from 1 to 28, as said below
- kv_cache: bfloat16 [2112, 8, 70, 256], P('owner', 'ingest'), may hold values from -250 to 250
- conv_cache: bfloat16 [2112, 8, 1024], P('owner', None, 'ingest'), may hold values from -5 to 5
- mig_owner: int32 [2048], P('owner'), may hold values from 0 to 63, as said below
- ln1_gain: float32 [1024], replicated, may hold values from 0.1 to 1.9
- w_qkv: bfloat16 [1024, 8, 384], P(None, 'ingest'), may hold values from -0.1875 to 0.1875
- w_out: bfloat16 [1024, 1024], P('ingest'), may hold values from -0.1875 to 0.1875
- ln2_gain: float32 [1024], replicated, may hold values from 0.1 to 1.9
- w_pw1: bfloat16 [1024, 2, 1024], P(None, None, 'ingest'), may hold values from -0.1875 to 0.1875
- dw_weight: bfloat16 [9, 1024], P(None, 'ingest'), may hold values from -2 to 2
- bn_scale: float32 [1024], P('ingest'), may hold values from 0.1 to 1.9
- bn_shift: float32 [1024], P('ingest'), may hold values from -2.5 to 2.5
- w_pw2: bfloat16 [1024, 1024], P('ingest'), may hold values from -0.1875 to 0.1875
Outputs:
- layer_out: bfloat16 [2112, 28, 1024], P('owner', None, 'ingest')
- kv_next: bfloat16 [2112, 8, 70, 256], P('owner', 'ingest')
- conv_next: bfloat16 [2112, 8, 1024], P('owner', None, 'ingest')
Inputs may be any that keep to these rules, and one draw needn't show every extreme that they name: `route_owner`: every owner receives exactly 33 utterances. The utterances that one source device along owner (a block of 33 rows in arrival order) sends to one owner number at most 1, and some source device reaches that number. `route_slot`: the utterances sent to one owner have distinct slots. Every owner holds an utterance with 28 new frames. The utterance in old slot 1 + j of an owner moves to slot 1 + j of owner mig_owner; the 32 utterances of one owner go to 32 different other owners, and every owner receives exactly one utterance for each j.
All inputs are finite; a program needn't handle non-finite values.
Results may differ from a plain program's by a relative error of at most 0.01.
Values may be sent and summed in bfloat16 or wider, within the bound.
No kernel may reach another device: no remote copies, remote signals or barrier semaphores. Data moves between devices by JAX's collectives and lax.ppermute only.
A program may use at most 64 MiB of HBM per device.

v0:
```python
import jax
import jax.numpy as jnp
from jax import lax
from jax.sharding import PartitionSpec as P

BLOCKS = 2
norm_eps = 1e-05


def normalize(values, gain_cols):
    model_width = values.shape[-1]
    row_mean = jnp.sum(values, axis=-1, keepdims=True) / model_width
    spread = jnp.sum(values * values, axis=-1, keepdims=True) / model_width - row_mean * row_mean
    return ((values - row_mean) * lax.rsqrt(spread + norm_eps) * gain_cols).astype(jnp.bfloat16)


def one_hot_rows(table, rows):
    return jnp.dot(table.astype(jnp.bfloat16), rows, preferred_element_type=jnp.float32).astype(
        jnp.bfloat16
    )


def grouped_terms(left_groups, right_groups):
    terms = jnp.einsum(
        "grc,gcn->grn", left_groups, right_groups, preferred_element_type=jnp.float32
    ).astype(jnp.bfloat16)
    return jnp.sum(terms.astype(jnp.float32), axis=0)


def shards(
    frame_rows,
    route_owner,
    route_slot,
    frames,
    kv_cache,
    conv_cache,
    mig_owner,
    ln1_gain,
    w_qkv,
    w_out,
    ln2_gain,
    w_pw1,
    dw_weight,
    bn_scale,
    bn_shift,
    w_pw2,
):
    owners = lax.axis_size("owner")
    groups = lax.axis_size("ingest")
    me = lax.axis_index("ingest")
    utterances, frame_span, local_width = frame_rows.shape
    model_width = w_qkv.shape[0]
    head_dim = w_qkv.shape[2] // 3
    cache_len = kv_cache.shape[2]
    conv_len = conv_cache.shape[1]
    taps = dw_weight.shape[0]
    horizon = frame_span // BLOCKS
    moving = mig_owner.shape[0]
    settled = utterances - moving
    lanes = 128
    w_out_full = lax.all_gather(w_out, "ingest", axis=0, tiled=True)
    w_pw2_cols = lax.all_to_all(
        w_pw2.reshape(local_width, groups, local_width).transpose(1, 0, 2),
        "ingest",
        split_axis=0,
        concat_axis=0,
        tiled=True,
    )
    dest = jnp.arange(owners, dtype=jnp.int32)
    frame_flat = frame_rows.reshape(utterances, frame_span * local_width)
    slot_tag = jnp.broadcast_to((route_slot + 1).astype(jnp.bfloat16)[:, None], (utterances, lanes))
    frame_send = one_hot_rows(
        dest[:, None] == route_owner[None, :], jnp.concatenate([frame_flat, slot_tag], axis=1)
    )
    kv_width = cache_len * 2 * head_dim
    conv_width = conv_len * local_width
    mover_tag = jnp.broadcast_to(
        (jnp.arange(moving, dtype=jnp.int32) + 1).astype(jnp.bfloat16)[:, None], (moving, lanes)
    )
    cache_rows = jnp.concatenate(
        [
            kv_cache[settled:].reshape(moving, kv_width),
            conv_cache[settled:].reshape(moving, conv_width),
            mover_tag,
        ],
        axis=1,
    )
    cache_send = one_hot_rows(dest[:, None] == mig_owner[None, :], cache_rows)
    frame_cols = frame_send.shape[1]
    arrived = lax.all_to_all(
        jnp.concatenate([frame_send, cache_send], axis=1),
        "owner",
        split_axis=0,
        concat_axis=0,
        tiled=True,
    )
    frame_part = frame_span * local_width
    got_slot = arrived[:, frame_part].astype(jnp.int32)
    slots = jnp.arange(utterances, dtype=jnp.int32)
    arranged = one_hot_rows(
        slots[:, None] + 1 == got_slot[None, :], arrived[:, :frame_part]
    ).reshape(utterances, frame_span, local_width)
    got_mover = arrived[:, frame_cols + kv_width + conv_width].astype(jnp.int32)
    movers = jnp.arange(moving, dtype=jnp.int32)
    moved = one_hot_rows(
        movers[:, None] + 1 == got_mover[None, :],
        arrived[:, frame_cols : frame_cols + kv_width + conv_width],
    )
    kv_state = jnp.concatenate(
        [
            kv_cache[:settled].reshape(settled, cache_len, 2 * head_dim),
            moved[:, :kv_width].reshape(moving, cache_len, 2 * head_dim),
        ],
        axis=0,
    )
    conv_state = jnp.concatenate(
        [conv_cache[:settled], moved[:, kv_width:].reshape(moving, conv_len, local_width)], axis=0
    )
    x_all = lax.all_gather(arranged, "ingest", axis=0, tiled=False)
    x_rows = x_all.transpose(1, 2, 0, 3).reshape(utterances, frame_span, model_width)
    x_rows = x_rows.astype(jnp.float32)
    normed = normalize(x_rows, ln1_gain)
    projected = jnp.dot(
        normed, w_qkv.reshape(model_width, 3 * head_dim), preferred_element_type=jnp.float32
    )
    queries = projected[..., :head_dim].astype(jnp.bfloat16)
    fresh = projected[..., head_dim:].astype(jnp.bfloat16)
    memory = jnp.concatenate([kv_state, fresh], axis=1)
    keys_total = memory.shape[1]
    scores = jnp.einsum(
        "sqd,skd->sqk", queries, memory[..., :head_dim], preferred_element_type=jnp.float32
    ) * head_dim ** (-0.5)
    frame_index = jnp.arange(frame_span, dtype=jnp.int32)
    block_of = frame_index // horizon
    low = block_of * horizon
    high = cache_len + jnp.minimum(frames[:, None], (block_of[None, :] + 1) * horizon)
    position = jnp.arange(keys_total, dtype=jnp.int32)
    live_keys = (position[None, None, :] >= low[None, :, None]) & (
        position[None, None, :] < high[:, :, None]
    )
    scores = jnp.where(live_keys, scores, -1e30)
    row_max = jnp.max(scores, axis=-1, keepdims=True)
    weights = jnp.exp(scores - row_max)
    probabilities = (weights / jnp.sum(weights, axis=-1, keepdims=True)).astype(jnp.bfloat16)
    context = jnp.einsum(
        "sqk,skd->sqd", probabilities, memory[..., head_dim:], preferred_element_type=jnp.float32
    ).astype(jnp.bfloat16)
    ctx_all = lax.all_gather(context, "ingest", axis=0, tiled=False)
    row_count = utterances * frame_span
    attn = grouped_terms(
        ctx_all.reshape(groups, row_count, head_dim),
        w_out_full.reshape(groups, head_dim, model_width),
    )
    residual = x_rows.reshape(row_count, model_width) + attn
    normed2 = normalize(residual, ln2_gain)
    mixed = jnp.dot(
        normed2, w_pw1.reshape(model_width, 2 * local_width), preferred_element_type=jnp.float32
    )
    glu_out = (mixed[:, :local_width] * jax.nn.sigmoid(mixed[:, local_width:])).astype(jnp.bfloat16)
    glu_out = glu_out.reshape(utterances, frame_span, local_width)
    joined = jnp.concatenate([conv_state, glu_out], axis=1)
    joined_f = joined.astype(jnp.float32)
    running = jnp.zeros((utterances, frame_span, local_width), jnp.float32)
    for tap_index in range(taps):
        running = running + joined_f[:, tap_index : tap_index + frame_span, :] * dw_weight[
            tap_index
        ].astype(jnp.float32)
    activated = jax.nn.silu(running * bn_scale + bn_shift).astype(jnp.bfloat16)
    act_all = lax.all_gather(activated, "ingest", axis=0, tiled=False)
    conv_terms = grouped_terms(act_all.reshape(groups, row_count, local_width), w_pw2_cols)
    residual_own = lax.dynamic_slice_in_dim(residual, me * local_width, local_width, 1)
    result = (residual_own + conv_terms).reshape(utterances, frame_span, local_width)
    live_rows = frame_index[None, :] < frames[:, None]
    layer_out = jnp.where(live_rows[:, :, None], result, 0.0).astype(jnp.bfloat16)
    keep = jnp.arange(cache_len, dtype=jnp.int32)
    kv_pick = position[None, None, :] == keep[None, :, None] + frames[:, None, None]
    kv_next = jnp.einsum(
        "srp,spd->srd", kv_pick.astype(jnp.bfloat16), memory, preferred_element_type=jnp.float32
    ).astype(jnp.bfloat16)
    conv_keep = jnp.arange(conv_len, dtype=jnp.int32)
    conv_pos = jnp.arange(joined.shape[1], dtype=jnp.int32)
    conv_pick = conv_pos[None, None, :] == conv_keep[None, :, None] + frames[:, None, None]
    conv_next = jnp.einsum(
        "srp,spd->srd", conv_pick.astype(jnp.bfloat16), joined, preferred_element_type=jnp.float32
    ).astype(jnp.bfloat16)
    return (layer_out, kv_next.reshape(kv_cache.shape), conv_next)


def solution(mesh):
    in_specs = (
        P("owner", None, "ingest"),
        P("owner"),
        P("owner"),
        P("owner"),
        P("owner", "ingest", None, None),
        P("owner", None, "ingest"),
        P("owner"),
        P(),
        P(None, "ingest", None),
        P("ingest", None),
        P(),
        P(None, None, "ingest"),
        P(None, "ingest"),
        P("ingest"),
        P("ingest"),
        P("ingest", None),
    )
    out_specs = (
        P("owner", None, "ingest"),
        P("owner", "ingest", None, None),
        P("owner", None, "ingest"),
    )
    return jax.shard_map(shards, mesh=mesh, in_specs=in_specs, out_specs=out_specs, check_vma=False)
```

profile of v0, /device:TPU:1, one launch (start us, length us, event | category | flops | bytes accessed | tf_op | source)
XLA Modules:
  0.0 387.9 jit_solution(17638379592714041639)
XLA Ops:
  7.3 1.5 slice-done
  8.8 0.2 copy.37
  9.3 0.3 convolution_convert_fusion.2
  9.7 0.8 convolution_convert_fusion
  10.5 1.8 maximum_bitcast_fusion
  12.3 0.5 broadcast.254
  12.8 5.4 %reduce.8 = bf16[64,22784]{1,0:T(8,128)(2,1)} reduce(bf16[64,1,22784]{2,0,1:T(8,128)(2,1)} %maximum_bitcast_fusion, bf16[]{:T(256)} %broadcast.254), dimensions={1}, to_apply=%copy.30.reduce_sub_computation | reduce | bytes 5832706 | tf_op jit(solution)/shard_map/all_to_all | solution.py:90
  18.2 4.4 %reshape.407 = bf16[64,2,11392]{2,1,0:T(2,128)(2,1)} reshape(bf16[64,22784]{1,0:T(8,128)(2,1)} %reduce.8) | data formatting | bytes 5832704
  22.6 19.3 %all-to-all-start = ((bf16[64,2,11392]{2,1,0:T(2,128)(2,1)}), bf16[64,2,11392]{2,1,0:T(2,128)(2,1)}, u32[]{:S(2)}, u32[]{:S(2)}) async-start(bf16[64,2,11392]{2,1,0:T(2,128)(2,1)} %reshape.407), calls=%async_computation | async-start | bytes 5832704 | tf_op jit(solution)/shard_map/all_to_all | solution.py:90
  42.0 127.4 %all-to-all-done = bf16[64,2,11392]{2,1,0:T(2,128)(2,1)} async-done(((bf16[64,2,11392]{2,1,0:T(2,128)(2,1)}), bf16[64,2,11392]{2,1,0:T(2,128)(2,1)}, u32[]{:S(2)}, u32[]{:S(2)}) %all-to-all-start) | async-done | bytes 2916384 | tf_op jit(solution)/shard_map/all_to_all | solution.py:90
  169.5 16.8 %reshape.408 = bf16[64,1,22784]{2,1,0:T(2,128)(2,1)} reshape(bf16[64,2,11392]{2,1,0:T(2,128)(2,1)} %all-to-all-done) | data formatting | bytes 5832704
  186.2 3.1 copy.57
  189.4 1.5 copy-done.3
  190.9 0.3 convolution_convert_fusion.3
  191.2 0.9 all_gather_reshape.3
  192.1 0.2 all-gather.11.cloned.1.call-start
  192.5 2.2 convolution_convert_fusion.1
  194.7 1.2 slice.143
  195.9 2.5 reshape.378
  198.4 26.5 %all-gather.7.cloned.1.call-done = bf16[8,33,28,128]{3,2,1,0:T(8,128)(2,1)} async-done(((bf16[1,33,28,128]{3,2,1,0:T(8,128)(2,1)}), bf16[8,33,28,128]{3,2,1,0:T(8,128)(2,1)}) %all-gather.7.cloned.1.call-update) | async-done | bytes 1892368 | tf_op jit(solution)/shard_map/all_gather | solution.py:119
  224.9 5.3 %bitcast_reduce_fusion = (f32[33,28]{1,0:T(8,128)S(1)}, f32[33,28]{1,0:T(8,128)S(1)}) fusion(bf16[8,33,28,128]{3,2,1,0:T(8,128)(2,1)} %all-gather.7.cloned.1.call-done), kind=kLoop, calls=%fused_computation.9 | loop fusion | flops 3782856 | bytes 1899744 | tf_op jit(solution)/shard_map/reduce_sum | solution.py:12
  230.3 5.5 %fusion.3 = bf16[33,28,8,128]{3,2,1,0:T(8,128)(2,1)} fusion(f32[8,128]{1,0:T(8,128)S(1)} %bitcast.128, f32[33,28]{1,0:T(8,128)S(1)} %get-tuple-element.24, f32[33,28]{1,0:T(8,128)S(1)} %get-tuple-element.23, bf16[8,33,28,128]{3,2,1,0:T(8,128)(2,1)S(1)} %copy-done.2), kind=kLoop, calls=%fused_computation.13 | loop fusion | flops 4730880 | bytes 3796192 | tf_op jit(solution)/shard_map/convert_element_type | solution.py:14
  235.7 4.1 %convert_element_type.219 = bf16[33,28,1024]{2,1,0:T(8,128)(2,1)} reshape(bf16[33,28,8,128]{3,2,1,0:T(8,128)(2,1)} %fusion.3) | data formatting | bytes 3784704 | tf_op jit(solution)/shard_map/convert_element_type | solution.py:14
  239.9 3.0 convolution_convert_fusion.5
  242.9 0.3 pad_maximum_fusion
  243.3 1.2 copy-done.9
  244.5 0.6 fusion.10
  245.1 0.4 fusion.61
  245.5 3.8 convolution_convert_fusion.6
  249.3 0.7 all-gather.9.cloned.1.call-update
  250.0 0.3 all-gather.13.cloned.1.call-start
  250.3 0.6 bitcast_convert_fusion.8
  250.9 0.8 slice_bitcast_fusion
  251.8 31.2 %all-gather.11.cloned.1.call-done = bf16[264,28,128]{2,1,0:T(8,128)(2,1)} async-done(((bf16[33,28,128]{2,1,0:T(8,128)(2,1)}), bf16[264,28,128]{2,1,0:T(8,128)(2,1)}) %all-gather.11.cloned.1.call-update) | async-done | bytes 1892368 | tf_op jit(solution)/shard_map/all_gather | solution.py:148
  283.0 3.6 reshape.379
  286.6 32.0 %all-gather.9.cloned.1.call-done = bf16[1024,1024]{1,0:T(8,128)(2,1)} async-done(((bf16[128,1024]{1,0:T(8,128)(2,1)}), bf16[1024,1024]{1,0:T(8,128)(2,1)}) %all-gather.9.cloned.1.call-update) | async-done | bytes 2097168 | tf_op jit(solution)/shard_map/all_gather | solution.py:61
  318.6 6.6 %convert_reduce_fusion = f32[924,1024]{1,0:T(8,128)S(1)} fusion(bf16[8,924,128]{2,1,0:T(8,128)(2,1)} %reshape.379, bf16[8,128,1024]{2,1,0:T(8,128)(2,1)} %bitcast.129), kind=kOutput, calls=%fused_computation.1 | convolution fusion | flops 1959530496 | bytes 7774208 | tf_op jit(solution)/shard_map/grc,gcn->grn/dot_general | solution.py:24
  325.3 0.9 copy.41
  326.2 1.0 copy-done.5
  327.2 0.2 slice.159
  327.5 3.6 fusion.6
  331.1 5.0 %multiply_convert_fusion = bf16[33,28,8,128]{3,2,1,0:T(8,128)(2,1)S(1)} fusion(f32[8,128]{1,0:T(8,128)S(1)} %bitcast.127, f32[33,28]{1,0:T(8,128)S(1)} %get-tuple-element.22, f32[33,28]{1,0:T(8,128)S(1)} %get-tuple-element.21, f32[33,28,8,128]{3,2,1,0:T(8,128)S(1)} %bitcast.106, bf16[8,33,28,128]{3,2,1,0:T(8,128)(2,1)S(1)} %copy-done.2), kind=kLoop, calls=%fused_computation.15 | loop fusion | flops 5677056 | bytes 7580896 | tf_op jit(solution)/shard_map/convert_element_type | solution.py:14
  336.1 0.1 pad.15
  336.3 0.6 copy.42
  336.8 0.5 copy-done.25
  337.3 0.7 fusion.31
  338.0 0.1 fusion.39
  338.2 0.7 reshape.383
  338.9 1.0 fusion.46
  340.0 1.4 multiply_convert_fusion.1
  341.4 1.1 copy.32
  342.5 0.9 copy.33
  343.4 4.3 %all-to-all-start.1 = ((bf16[8,128,128]{2,1,0:T(8,128)(2,1)}), bf16[8,128,128]{2,1,0:T(8,128)(2,1)}, u32[]{:S(2)}, u32[]{:S(2)}) async-start(bf16[8,128,128]{2,1,0:T(8,128)(2,1)} %bitcast.18), calls=%async_computation.1 | async-start | bytes 524288 | tf_op jit(solution)/shard_map/all_to_all | solution.py:62
  347.9 0.9 copy_convert_fusion
  348.8 0.4 copy-done.7
  349.2 1.9 fusion.7
  351.1 0.2 pad.14
  351.4 2.8 copy.39
  354.1 0.9 convolution_convert_fusion.7
  355.0 19.9 %all-gather.13.cloned.1.call-done = bf16[264,28,128]{2,1,0:T(8,128)(2,1)} async-done(((bf16[33,28,128]{2,1,0:T(8,128)(2,1)}), bf16[264,28,128]{2,1,0:T(8,128)(2,1)}) %all-gather.13.cloned.1.call-update) | async-done | bytes 1892368 | tf_op jit(solution)/shard_map/all_gather | solution.py:169
  374.9 2.5 reshape.384
  377.5 1.6 convert_reduce_fusion.1
  379.1 1.3 fusion.38
  380.4 0.9 select_convert_fusion
  (81 shorter events, 1.2 us)
Async XLA Ops:
  7.2 232.7 %copy-start = (bf16[1024,1,384]{2,0,1:T(8,128)(2,1)S(1)}, bf16[1024,1,384]{2,0,1:T(8,128)(2,1)}, u32[]{:S(2)}) copy-start(bf16[1024,1,384]{2,0,1:T(8,128)(2,1)} %param.24) | copy-start | bytes 2359300
  7.2 1.6 slice-start
  7.2 1.9 slice-start.1
  7.2 1.9 copy-start.11
  7.2 2.0 copy-start.26
  7.2 2.1 copy-start.23
  7.3 2.5 copy-start.24
  22.6 146.9 %all-to-all-start = ((bf16[64,2,11392]{2,1,0:T(2,128)(2,1)}), bf16[64,2,11392]{2,1,0:T(2,128)(2,1)}, u32[]{:S(2)}, u32[]{:S(2)}) async-start(bf16[64,2,11392]{2,1,0:T(2,128)(2,1)} %reshape.407), calls=%async_computation | async-start | bytes 5832704 | tf_op jit(solution)/shard_map/all_to_all | solution.py:90
  42.0 182.9 %all-gather.7.cloned.1.call-start = ((), (), s32[]{:S(2)}) async-start(), calls=%async_computation.2 | async-start | bytes 2433024 | tf_op jit(solution)/shard_map/all_gather | solution.py:119
  186.2 6.2 %copy-start.13 = (s32[33]{0:T(128)S(1)}, s32[33]{0:T(128)}, u32[]{:S(2)}) copy-start(s32[33]{0:T(128)} %param.19) | copy-start | bytes 400
  186.2 6.2 %copy-start.8 = (bf16[33,1,70,256]{3,2,1,0:T(8,128)(2,1)S(1)}, bf16[33,1,70,256]{3,2,1,0:T(8,128)(2,1)}, u32[]{:S(2)}) copy-start(bf16[33,1,70,256]{3,2,1,0:T(8,128)(2,1)} %param.20) | copy-start | bytes 3548164
  189.3 1.6 copy-start.3
  192.1 90.9 %all-gather.11.cloned.1.call-start = ((), (), s32[]{:S(2)}) async-start(), calls=%async_computation.4 | async-start | bytes 2433024 | tf_op jit(solution)/shard_map/all_gather | solution.py:148
  194.7 3.7 copy-start.4
  195.9 34.4 %copy-start.16 = (f32[1024]{0:T(1024)S(1)}, f32[1024]{0:T(1024)}, u32[]{:S(2)}) copy-start(f32[1024]{0:T(1024)} %param.23) | copy-start | bytes 12292
  224.9 5.4 %copy-start.2 = (bf16[8,33,28,128]{3,2,1,0:T(8,128)(2,1)S(1)}, bf16[8,33,28,128]{3,2,1,0:T(8,128)(2,1)}, u32[]{:S(2)}) copy-start(bf16[8,33,28,128]{3,2,1,0:T(8,128)(2,1)} %all-gather.7.cloned.1.call-done) | copy-start | bytes 5677060
  239.9 3.1 copy-start.6
  243.3 1.2 copy-start.9
  245.1 5.2 %copy-start.12 = (bf16[33,8,128]{2,1,0:T(8,128)(2,1)S(1)}, bf16[33,8,128]{2,1,0:T(8,128)(2,1)}, u32[]{:S(2)}) copy-start(bf16[33,8,128]{2,1,0:T(8,128)(2,1)} %param.21) | copy-start | bytes 202756
  245.1 5.2 %copy-start.14 = (bf16[9,128]{1,0:T(8,128)(2,1)S(1)}, bf16[9,128]{1,0:T(8,128)(2,1)}, u32[]{:S(2)}) copy-start(bf16[9,128]{1,0:T(8,128)(2,1)} %param.28) | copy-start | bytes 6916
  249.3 69.4 %all-gather.9.cloned.1.call-start = ((), (), s32[]{:S(2)}) async-start(), calls=%async_computation.3 | async-start | bytes 2359296 | tf_op jit(solution)/shard_map/all_gather | solution.py:61
  250.0 124.9 %all-gather.13.cloned.1.call-start = ((), (), s32[]{:S(2)}) async-start(), calls=%async_computation.5 | async-start | bytes 2433024 | tf_op jit(solution)/shard_map/all_gather | solution.py:169
  325.3 1.9 copy-start.5
  327.4 3.6 copy-start.15
  336.3 1.0 copy-start.25
  338.0 2.0 copy-start.17
  338.0 2.0 copy-start.18
  338.0 2.0 copy-start.19
  338.0 2.0 copy-start.20
  338.0 2.0 copy-start.21
  338.0 2.0 copy-start.22
  343.4 34.0 %all-to-all-start.1 = ((bf16[8,128,128]{2,1,0:T(8,128)(2,1)}), bf16[8,128,128]{2,1,0:T(8,128)(2,1)}, u32[]{:S(2)}, u32[]{:S(2)}) async-start(bf16[8,128,128]{2,1,0:T(8,128)(2,1)} %bitcast.18), calls=%async_computation.1 | async-start | bytes 524288 | tf_op jit(solution)/shard_map/all_to_all | solution.py:62
  347.9 1.3 copy-start.7
  351.3 2.8 copy-start.10
  374.9 6.4 %copy-start.1 = (bf16[1024,1,384]{2,0,1:T(8,128)(2,1)S(1)}, bf16[1024,1,384]{2,0,1:T(8,128)(2,1)}, u32[]{:S(2)}) copy-start(bf16[1024,1,384]{2,0,1:T(8,128)(2,1)} %param.24) | copy-start | bytes 2359300
Sparse Core Ops, SparseCore 0:
  192.2 32.6 all-gather.6
  249.4 33.5 all-gather.10
  285.2 33.4 all-gather.8
  341.5 33.3 all-gather.12
where the time goes:
time: 389 us; the launch traced here: 388 us
  waiting for transfers between devices  238 us (61%)
  local copies, waits for them, and re-layouts  54.9 us (14%)
  other arithmetic  34 us (9%)
  starting transfers between devices  24.2 us (6%)
  matrix products  22.6 us (6%)
  between operations  14.4 us (4%)
    all_to_all x1, waiting for transfers between devices, shards(): lax.all_to_all(jnp.concatenate([frame_send, cache_send], axis=1), 'owner'...  127 us
    unnamed x70, local copies, waits for them, and re-layouts  36.2 us
    all_gather x1, waiting for transfers between devices, shards(): w_out_full = lax.all_gather(w_out, 'ingest', axis=0, tiled=True)  32 us
    all_gather x1, waiting for transfers between devices, shards(): ctx_all = lax.all_gather(context, 'ingest', axis=0, tiled=False)  31.2 us
    all_gather x1, waiting for transfers between devices, shards(): x_all = lax.all_gather(arranged, 'ingest', axis=0, tiled=False)  26.5 us
    all_gather x1, waiting for transfers between devices, shards(): act_all = lax.all_gather(activated, 'ingest', axis=0, tiled=False)  19.9 us
    all_to_all x1, starting transfers between devices, shards(): lax.all_to_all(jnp.concatenate([frame_send, cache_send], axis=1), 'owner'...  19.3 us
    convert_element_type x2, other arithmetic, normalize(): ((values - row_mean) * lax.rsqrt(spread + norm_eps) * gain_cols).astype(j...  10.5 us
  transfers between devices with their start and end apart: 6, of which 5 were waited for; matrix products, arithmetic and copies ran while one was open for 6% of the time, Pallas kernels for 0%

commit v1 on v0

--- a/solution.py
+++ b/solution.py
@@ -58,7 +58,14 @@
     moving = mig_owner.shape[0]
     settled = utterances - moving
     lanes = 128
-    w_out_full = lax.all_gather(w_out, "ingest", axis=0, tiled=True)
+    ring = [w_out]
+    for hop in range(7):
+        ring.append(lax.ppermute(ring[-1], "ingest", [(dev, (dev + 1) % 8) for dev in range(8)]))
+    w_out_full = jnp.roll(
+        jnp.concatenate(ring[::-1], axis=0),
+        (lax.axis_index("ingest") + 1) * ring[0].shape[0],
+        axis=0,
+    )
     w_pw2_cols = lax.all_to_all(
         w_pw2.reshape(local_width, groups, local_width).transpose(1, 0, 2),
         "ingest",

time: 389 us -> 362 us (0.931)
  waiting for transfers between devices: 238 us -> 170 us
  starting transfers between devices: 24.2 us -> 51 us
  local copies, waits for them, and re-layouts: 54.9 us -> 67.4 us
    all_gather x1 -> x0, waiting for transfers between devices: 32 us -> none  [shards(): w_out_full = lax.all_gather(w_out, 'ingest', axis=0, tiled=True)]
    all_gather x1, waiting for transfers between devices: 31.2 us -> 1.87 us  [shards(): ctx_all = lax.all_gather(context, 'ingest', axis=0, tiled=False)]
    ppermute x0 -> x7, waiting for transfers between devices: none -> 28.8 us  [shards(): lax.ppermute(ring[-1], 'ingest', [(dev, (dev + 1) % 8) for dev in range(8)])]
    all_gather x1, waiting for transfers between devices: 26.5 us -> 0.01 us  [shards(): x_all = lax.all_gather(arranged, 'ingest', axis=0, tiled=False)]
    ppermute x0 -> x7, starting transfers between devices: none -> 17.6 us  [shards(): lax.ppermute(ring[-1], 'ingest', [(dev, (dev + 1) % 8) for dev in range(8)])]
    unnamed x70 -> x105, local copies, waits for them, and re-layouts: 36.2 us -> 46.4 us
    all_to_all x1, starting transfers between devices: 4.26 us -> 13.7 us  [shards(): lax.all_to_all(w_pw2.reshape(local_width, groups, local_width).transpose(...]
    all_gather x1, waiting for transfers between devices: 19.9 us -> 11.7 us  [shards(): act_all = lax.all_gather(activated, 'ingest', axis=0, tiled=False)]
  transfers between devices with their start and end apart: 6 -> 12, of which waited for: 5 -> 9; matrix products, arithmetic and copies ran while one was open for 6% -> 15% of each run, Pallas kernels for 0% -> 0%
where the time goes in v1:
time: 362 us; the launch traced here: 360 us
  waiting for transfers between devices  170 us (47%)
  local copies, waits for them, and re-layouts  67.4 us (19%)
  starting transfers between devices  51 us (14%)
  other arithmetic  34.6 us (10%)
  matrix products  23 us (6%)
  between operations  14.5 us (4%)
    all_to_all x1, waiting for transfers between devices, shards(): lax.all_to_all(jnp.concatenate([frame_send, cache_send], axis=1), 'owner'...  127 us
    unnamed x105, local copies, waits for them, and re-layouts  46.4 us
    ppermute x7, waiting for transfers between devices, shards(): lax.ppermute(ring[-1], 'ingest', [(dev, (dev + 1) % 8) for dev in range(8)])  28.8 us
    all_to_all x1, starting transfers between devices, shards(): lax.all_to_all(jnp.concatenate([frame_send, cache_send], axis=1), 'owner'...  19.3 us
    ppermute x7, starting transfers between devices, shards(): lax.ppermute(ring[-1], 'ingest', [(dev, (dev + 1) % 8) for dev in range(8)])  17.6 us
    all_to_all x1, starting transfers between devices, shards(): lax.all_to_all(w_pw2.reshape(local_width, groups, local_width).transpose(...  13.7 us
    all_gather x1, waiting for transfers between devices, shards(): act_all = lax.all_gather(activated, 'ingest', axis=0, tiled=False)  11.7 us
    convert_element_type x2, other arithmetic, normalize(): ((values - row_mean) * lax.rsqrt(spread + norm_eps) * gain_cols).astype(j...  10.5 us
  transfers between devices with their start and end apart: 12, of which 9 were waited for; matrix products, arithmetic and copies ran while one was open for 15% of the time, Pallas kernels for 0%

profile of v1, /device:TPU:1, one launch (start us, length us, event | category | flops | bytes accessed | tf_op | source)
XLA Modules:
  0.0 360.3 jit_solution(15492153064072090615)
XLA Ops:
  7.3 1.5 slice-done
  10.5 1.8 maximum_bitcast_fusion
  12.8 5.4 %reduce.8 = bf16[64,22784]{1,0:T(8,128)(2,1)} reduce(bf16[64,1,22784]{2,0,1:T(8,128)(2,1)} %maximum_bitcast_fusion, bf16[]{:T(256)} %broadcast.255), dimensions={1}, to_apply=%copy.30.reduce_sub_computation | reduce | bytes 5832706 | tf_op jit(solution)/shard_map/all_to_all | solution.py:97
  18.2 4.4 %reshape.407 = bf16[64,2,11392]{2,1,0:T(2,128)(2,1)} reshape(bf16[64,22784]{1,0:T(8,128)(2,1)} %reduce.8) | data formatting | bytes 5832704
  22.6 19.3 %all-to-all-start = ((bf16[64,2,11392]{2,1,0:T(2,128)(2,1)}), bf16[64,2,11392]{2,1,0:T(2,128)(2,1)}, u32[]{:S(2)}, u32[]{:S(2)}) async-start(bf16[64,2,11392]{2,1,0:T(2,128)(2,1)} %reshape.407), calls=%async_computation | async-start | bytes 5832704 | tf_op jit(solution)/shard_map/all_to_all | solution.py:97
  42.0 127.4 %all-to-all-done = bf16[64,2,11392]{2,1,0:T(2,128)(2,1)} async-done(((bf16[64,2,11392]{2,1,0:T(2,128)(2,1)}), bf16[64,2,11392]{2,1,0:T(2,128)(2,1)}, u32[]{:S(2)}, u32[]{:S(2)}) %all-to-all-start) | async-done | bytes 2916384 | tf_op jit(solution)/shard_map/all_to_all | solution.py:97
  169.5 16.7 %reshape.408 = bf16[64,1,22784]{2,1,0:T(2,128)(2,1)} reshape(bf16[64,2,11392]{2,1,0:T(2,128)(2,1)} %all-to-all-done) | data formatting | bytes 5832704
  186.2 3.1 copy.57
  189.4 1.5 copy-done.3
  191.2 0.9 all_gather_reshape.3
  192.3 8.3 %collective-permute-start = (bf16[128,1024]{1,0:T(8,128)(2,1)S(1)}, bf16[128,1024]{1,0:T(8,128)(2,1)S(1)}, u32[]{:S(2)}, u32[]{:S(2)}) collective-permute-start(bf16[128,1024]{1,0:T(8,128)(2,1)S(1)} %copy-done.11), channel_id=1, source_target_pairs={{0,64},{64,128},{128,192},{192,256},{256,320},{320,384},{384,448},... | collective-permute-start | bytes 786440 | tf_op jit(solution)/shard_map/ppermute | solution.py:63
  200.6 3.3 collective-permute-done
  203.9 2.5 collective-permute-start.1
  207.2 2.8 collective-permute-done.1
  210.0 2.5 collective-permute-start.2
  212.5 5.5 %collective-permute-done.2 = bf16[128,1024]{1,0:T(8,128)(2,1)} collective-permute-done((bf16[128,1024]{1,0:T(8,128)(2,1)S(1)}, bf16[128,1024]{1,0:T(8,128)(2,1)}, u32[]{:S(2)}, u32[]{:S(2)}) %collective-permute-start.2) | collective-permute-done | bytes 262176 | tf_op jit(solution)/shard_map/ppermute | solution.py:63
  217.9 2.6 collective-permute-start.3
  220.5 2.2 convolution_convert_fusion.1
  222.8 1.2 slice.143
  224.0 2.5 reshape.378
  226.5 5.3 %bitcast_reduce_fusion = (f32[33,28]{1,0:T(8,128)S(1)}, f32[33,28]{1,0:T(8,128)S(1)}) fusion(bf16[8,33,28,128]{3,2,1,0:T(8,128)(2,1)} %all-gather.6.cloned.1.call-done), kind=kLoop, calls=%fused_computation.9 | loop fusion | flops 3782856 | bytes 1899744 | tf_op jit(solution)/shard_map/reduce_sum | solution.py:12
  231.9 5.5 %fusion.3 = bf16[33,28,8,128]{3,2,1,0:T(8,128)(2,1)} fusion(f32[8,128]{1,0:T(8,128)S(1)} %bitcast.129, f32[33,28]{1,0:T(8,128)S(1)} %get-tuple-element.24, f32[33,28]{1,0:T(8,128)S(1)} %get-tuple-element.23, bf16[8,33,28,128]{3,2,1,0:T(8,128)(2,1)S(1)} %copy-done.2), kind=kLoop, calls=%fused_computation.13 | loop fusion | flops 4730880 | bytes 3796192 | tf_op jit(solution)/shard_map/convert_element_type | solution.py:14
  237.4 4.1 %convert_element_type.219 = bf16[33,28,1024]{2,1,0:T(8,128)(2,1)} reshape(bf16[33,28,8,128]{3,2,1,0:T(8,128)(2,1)} %fusion.3) | data formatting | bytes 3784704 | tf_op jit(solution)/shard_map/convert_element_type | solution.py:14
  241.5 3.0 convolution_convert_fusion.5
  244.9 1.2 copy-done.9
  246.7 0.8 copy-done.19
  247.9 4.2 %convolution_convert_fusion.6 = bf16[33,28,128]{2,1,0:T(8,128)(2,1)} fusion(bf16[33,98,256]{2,1,0:T(8,128)(2,1)} %copy-done.9, f32[33,28]{1,0:T(8,128)S(1)} %fusion.61, f32[33,28,98]{2,1,0:T(8,128)} %copy-done.19), kind=kOutput, calls=%fused_computation.35 | convolution fusion | flops 23572260 | bytes 2200176 | tf_op jit(solution)/shard_map/sqk,skd->sqd/dot_general | solution.py:152
  252.2 0.8 collective-permute-start.4
  253.0 5.0 %collective-permute-done.4 = bf16[128,1024]{1,0:T(8,128)(2,1)S(1)} collective-permute-done((bf16[128,1024]{1,0:T(8,128)(2,1)}, bf16[128,1024]{1,0:T(8,128)(2,1)S(1)}, u32[]{:S(2)}, u32[]{:S(2)}) %collective-permute-start.4) | collective-permute-done | bytes 262176 | tf_op jit(solution)/shard_map/ppermute | solution.py:63
  258.7 1.0 collective-permute-start.5
  259.7 6.2 %collective-permute-done.5 = bf16[128,1024]{1,0:T(8,128)(2,1)} collective-permute-done((bf16[128,1024]{1,0:T(8,128)(2,1)S(1)}, bf16[128,1024]{1,0:T(8,128)(2,1)}, u32[]{:S(2)}, u32[]{:S(2)}) %collective-permute-start.5) | collective-permute-done | bytes 262176 | tf_op jit(solution)/shard_map/ppermute | solution.py:63
  267.1 6.0 %collective-permute-done.6 = bf16[128,1024]{1,0:T(8,128)(2,1)} collective-permute-done((bf16[128,1024]{1,0:T(8,128)(2,1)}, bf16[128,1024]{1,0:T(8,128)(2,1)}, u32[]{:S(2)}, u32[]{:S(2)}) %collective-permute-start.6) | collective-permute-done | bytes 262176 | tf_op jit(solution)/shard_map/ppermute | solution.py:63
  273.1 1.0 constant_dynamic-update-slice_fusion.15
  274.1 1.0 constant_dynamic-update-slice_fusion.14
  275.1 1.0 constant_dynamic-update-slice_fusion.13
  276.1 1.0 constant_dynamic-update-slice_fusion.12
  277.0 1.0 constant_dynamic-update-slice_fusion.11
  278.1 1.0 constant_dynamic-update-slice_fusion.7
  279.1 1.0 constant_dynamic-update-slice_fusion.6
  280.1 1.0 constant_dynamic-update-slice_fusion.4
  281.1 1.0 constant_dynamic-update-slice_fusion.3
  282.1 1.5 constant_dynamic-slice_fusion
  283.6 0.8 slice_bitcast_fusion
  284.5 1.9 all-gather.8.cloned.1.call-done
  286.4 3.7 %reshape.379 = bf16[8,924,128]{2,1,0:T(8,128)(2,1)} reshape(bf16[264,28,128]{2,1,0:T(8,128)(2,1)} %all-gather.8.cloned.1.call-done) | data formatting | bytes 3784704 | tf_op jit(solution)/shard_map/reshape | solution.py:158
  290.0 6.6 %convert_reduce_fusion = f32[924,1024]{1,0:T(8,128)S(1)} fusion(bf16[8,924,128]{2,1,0:T(8,128)(2,1)} %reshape.379, bf16[8,128,1024]{2,1,0:T(8,128)(2,1)} %bitcast.119), kind=kOutput, calls=%fused_computation.1 | convolution fusion | flops 1959530496 | bytes 7774208 | tf_op jit(solution)/shard_map/grc,gcn->grn/dot_general | solution.py:24
  296.7 0.9 copy.41
  297.6 1.0 copy-done.5
  298.8 3.6 fusion.6
  302.5 5.0 %multiply_convert_fusion = bf16[33,28,8,128]{3,2,1,0:T(8,128)(2,1)S(1)} fusion(f32[8,128]{1,0:T(8,128)S(1)} %bitcast.128, f32[33,28]{1,0:T(8,128)S(1)} %get-tuple-element.22, f32[33,28]{1,0:T(8,128)S(1)} %get-tuple-element.21, f32[33,28,8,128]{3,2,1,0:T(8,128)S(1)} %bitcast.106, bf16[8,33,28,128]{3,2,1,0:T(8,128)(2,1)S(1)} %copy-done.2), kind=kLoop, calls=%fused_computation.15 | loop fusion | flops 5677056 | bytes 7580896 | tf_op jit(solution)/shard_map/convert_element_type | solution.py:14
  310.2 1.0 fusion.46
  311.2 1.4 multiply_convert_fusion.1
  312.7 1.1 copy.32
  313.8 0.9 copy.33
  314.6 13.7 %all-to-all-start.1 = ((bf16[8,128,128]{2,1,0:T(8,128)(2,1)}), bf16[8,128,128]{2,1,0:T(8,128)(2,1)}, u32[]{:S(2)}, u32[]{:S(2)}) async-start(bf16[8,128,128]{2,1,0:T(8,128)(2,1)} %bitcast.18), calls=%async_computation.1 | async-start | bytes 524288 | tf_op jit(solution)/shard_map/all_to_all | solution.py:69
  328.5 0.9 copy_convert_fusion
  329.9 1.9 fusion.7
  332.0 2.7 copy.39
  334.8 0.9 convolution_convert_fusion.7
  335.7 11.7 %all-gather.10.cloned.1.call-done = bf16[264,28,128]{2,1,0:T(8,128)(2,1)} async-done(((bf16[33,28,128]{2,1,0:T(8,128)(2,1)}), bf16[264,28,128]{2,1,0:T(8,128)(2,1)}) %all-gather.10.cloned.1.call-update) | async-done | bytes 1892368 | tf_op jit(solution)/shard_map/all_gather | solution.py:176
  347.4 2.5 reshape.384
  350.0 1.6 convert_reduce_fusion.1
  351.6 1.3 fusion.38
  352.9 0.9 select_convert_fusion
  (129 shorter events, 11.1 us)
Async XLA Ops:
  7.2 234.3 %copy-start = (bf16[1024,1,384]{2,0,1:T(8,128)(2,1)S(1)}, bf16[1024,1,384]{2,0,1:T(8,128)(2,1)}, u32[]{:S(2)}) copy-start(bf16[1024,1,384]{2,0,1:T(8,128)(2,1)} %param.24) | copy-start | bytes 2359300
  7.2 1.6 slice-start
  7.2 1.9 slice-start.1
  7.2 1.9 copy-start.20
  7.2 2.0 copy-start.36
  7.2 2.1 copy-start.33
  7.3 2.5 copy-start.34
  22.6 146.9 %all-to-all-start = ((bf16[64,2,11392]{2,1,0:T(2,128)(2,1)}), bf16[64,2,11392]{2,1,0:T(2,128)(2,1)}, u32[]{:S(2)}, u32[]{:S(2)}) async-start(bf16[64,2,11392]{2,1,0:T(2,128)(2,1)} %reshape.407), calls=%async_computation | async-start | bytes 5832704 | tf_op jit(solution)/shard_map/all_to_all | solution.py:97
  42.0 184.5 %all-gather.6.cloned.1.call-start = ((), (), s32[]{:S(2)}) async-start(), calls=%async_computation.2 | async-start | bytes 2433024 | tf_op jit(solution)/shard_map/all_gather | solution.py:126
  186.2 6.1 %copy-start.11 = (bf16[128,1024]{1,0:T(8,128)(2,1)S(1)}, bf16[128,1024]{1,0:T(8,128)(2,1)}, u32[]{:S(2)}) copy-start(bf16[128,1024]{1,0:T(8,128)(2,1)} %param.25) | copy-start | bytes 786436
  186.2 20.9 %copy-start.21 = (s32[33]{0:T(128)S(1)}, s32[33]{0:T(128)}, u32[]{:S(2)}) copy-start(s32[33]{0:T(128)} %param.19) | copy-start | bytes 400
  186.2 26.3 %copy-start.8 = (bf16[33,1,70,256]{3,2,1,0:T(8,128)(2,1)S(1)}, bf16[33,1,70,256]{3,2,1,0:T(8,128)(2,1)}, u32[]{:S(2)}) copy-start(bf16[33,1,70,256]{3,2,1,0:T(8,128)(2,1)} %param.20) | copy-start | bytes 3548164
  189.3 1.6 copy-start.3
  192.0 94.3 %all-gather.8.cloned.1.call-start = ((), (), s32[]{:S(2)}) async-start(), calls=%async_computation.3 | async-start | bytes 2433024 | tf_op jit(solution)/shard_map/all_gather | solution.py:155
  192.3 11.7 %collective-permute-start = (bf16[128,1024]{1,0:T(8,128)(2,1)S(1)}, bf16[128,1024]{1,0:T(8,128)(2,1)S(1)}, u32[]{:S(2)}, u32[]{:S(2)}) collective-permute-start(bf16[128,1024]{1,0:T(8,128)(2,1)S(1)} %copy-done.11), channel_id=1, source_target_pairs={{0,64},{64,128},{128,192},{192,256},{256,320},{320,384},{384,448},... | collective-permute-start | bytes 786440 | tf_op jit(solution)/shard_map/ppermute | solution.py:63
  203.9 20.1 %copy-start.13 = (bf16[128,1024]{1,0:T(8,128)(2,1)}, bf16[128,1024]{1,0:T(8,128)(2,1)S(1)}, u32[]{:S(2)}) copy-start(bf16[128,1024]{1,0:T(8,128)(2,1)S(1)} %collective-permute-done) | copy-start | bytes 786436
  203.9 6.0 %collective-permute-start.1 = (bf16[128,1024]{1,0:T(8,128)(2,1)S(1)}, bf16[128,1024]{1,0:T(8,128)(2,1)S(1)}, u32[]{:S(2)}, u32[]{:S(2)}) collective-permute-start(bf16[128,1024]{1,0:T(8,128)(2,1)S(1)} %collective-permute-done), channel_id=1, source_target_pairs={{0,64},{64,128},{128,192},{192,256},{256,320},{320,384},{384,448},... | collective-permute-start | bytes 786440 | tf_op jit(solution)/shard_map/ppermute | solution.py:63
  210.0 14.0 %copy-start.15 = (bf16[128,1024]{1,0:T(8,128)(2,1)}, bf16[128,1024]{1,0:T(8,128)(2,1)S(1)}, u32[]{:S(2)}) copy-start(bf16[128,1024]{1,0:T(8,128)(2,1)S(1)} %collective-permute-done.1) | copy-start | bytes 786436
  210.0 8.0 %collective-permute-start.2 = (bf16[128,1024]{1,0:T(8,128)(2,1)S(1)}, bf16[128,1024]{1,0:T(8,128)(2,1)}, u32[]{:S(2)}, u32[]{:S(2)}) collective-permute-start(bf16[128,1024]{1,0:T(8,128)(2,1)S(1)} %collective-permute-done.1), channel_id=1, source_target_pairs={{0,64},{64,128},{128,192},{192,256},{256,320},{320,384},{384,448},... | collective-permute-start | bytes 786440 | tf_op jit(solution)/shard_map/ppermute | solution.py:63
  217.9 34.2 %collective-permute-start.3 = (bf16[128,1024]{1,0:T(8,128)(2,1)}, bf16[128,1024]{1,0:T(8,128)(2,1)}, u32[]{:S(2)}, u32[]{:S(2)}) collective-permute-start(bf16[128,1024]{1,0:T(8,128)(2,1)} %collective-permute-done.2), channel_id=1, source_target_pairs={{0,64},{64,128},{128,192},{192,256},{256,320},{320,384},{384,448},... | collective-permute-start | bytes 786440 | tf_op jit(solution)/shard_map/ppermute | solution.py:63
  222.7 3.8 %copy-start.4 = (bf16[32,18944]{1,0:T(8,128)(2,1)}, bf16[32,18944]{1,0:T(8,128)(2,1)S(1)}, u32[]{:S(2)}) copy-start(bf16[32,18944]{1,0:T(8,128)(2,1)S(1)} %convolution_convert_fusion.1) | copy-start | bytes 3637252
  222.8 9.1 %copy-start.24 = (f32[1024]{0:T(1024)S(1)}, f32[1024]{0:T(1024)}, u32[]{:S(2)}) copy-start(f32[1024]{0:T(1024)} %param.23) | copy-start | bytes 12292
  226.5 5.4 %copy-start.2 = (bf16[8,33,28,128]{3,2,1,0:T(8,128)(2,1)S(1)}, bf16[8,33,28,128]{3,2,1,0:T(8,128)(2,1)}, u32[]{:S(2)}) copy-start(bf16[8,33,28,128]{3,2,1,0:T(8,128)(2,1)} %all-gather.6.cloned.1.call-done) | copy-start | bytes 5677060
  241.5 3.1 copy-start.6
  244.5 1.7 copy-start.25
  244.9 1.2 copy-start.9
  246.1 20.4 %copy-start.22 = (bf16[9,128]{1,0:T(8,128)(2,1)S(1)}, bf16[9,128]{1,0:T(8,128)(2,1)}, u32[]{:S(2)}) copy-start(bf16[9,128]{1,0:T(8,128)(2,1)} %param.28) | copy-start | bytes 6916
  246.7 0.8 copy-start.19
  247.9 30.1 %copy-start.16 = (bf16[128,1024]{1,0:T(8,128)(2,1)S(1)}, bf16[128,1024]{1,0:T(8,128)(2,1)}, u32[]{:S(2)}) copy-start(bf16[128,1024]{1,0:T(8,128)(2,1)} %copy-done.15) | copy-start | bytes 786436
  247.9 30.2 %copy-start.14 = (bf16[128,1024]{1,0:T(8,128)(2,1)S(1)}, bf16[128,1024]{1,0:T(8,128)(2,1)}, u32[]{:S(2)}) copy-start(bf16[128,1024]{1,0:T(8,128)(2,1)} %copy-done.13) | copy-start | bytes 786436
  247.9 30.2 %copy-start.12 = (bf16[128,1024]{1,0:T(8,128)(2,1)S(1)}, bf16[128,1024]{1,0:T(8,128)(2,1)}, u32[]{:S(2)}) copy-start(bf16[128,1024]{1,0:T(8,128)(2,1)} %param.25) | copy-start | bytes 786436
  252.1 95.3 %all-gather.10.cloned.1.call-start = ((), (), s32[]{:S(2)}) async-start(), calls=%async_computation.4 | async-start | bytes 2433024 | tf_op jit(solution)/shard_map/all_gather | solution.py:176
  252.2 5.8 %collective-permute-start.4 = (bf16[128,1024]{1,0:T(8,128)(2,1)}, bf16[128,1024]{1,0:T(8,128)(2,1)S(1)}, u32[]{:S(2)}, u32[]{:S(2)}) collective-permute-start(bf16[128,1024]{1,0:T(8,128)(2,1)} %collective-permute-done.3), channel_id=1, source_target_pairs={{0,64},{64,128},{128,192},{192,256},{256,320},{320,384},{384,448},... | collective-permute-start | bytes 786440 | tf_op jit(solution)/shard_map/ppermute | solution.py:63
  258.0 0.7 copy-start.17
  258.7 7.1 %collective-permute-start.5 = (bf16[128,1024]{1,0:T(8,128)(2,1)S(1)}, bf16[128,1024]{1,0:T(8,128)(2,1)}, u32[]{:S(2)}, u32[]{:S(2)}) collective-permute-start(bf16[128,1024]{1,0:T(8,128)(2,1)S(1)} %collective-permute-done.4), channel_id=1, source_target_pairs={{0,64},{64,128},{128,192},{192,256},{256,320},{320,384},{384,448},... | collective-permute-start | bytes 786440 | tf_op jit(solution)/shard_map/ppermute | solution.py:63
  265.8 7.3 %collective-permute-start.6 = (bf16[128,1024]{1,0:T(8,128)(2,1)}, bf16[128,1024]{1,0:T(8,128)(2,1)}, u32[]{:S(2)}, u32[]{:S(2)}) collective-permute-start(bf16[128,1024]{1,0:T(8,128)(2,1)} %collective-permute-done.5), channel_id=1, source_target_pairs={{0,64},{64,128},{128,192},{192,256},{256,320},{320,384},{384,448},... | collective-permute-start | bytes 786440 | tf_op jit(solution)/shard_map/ppermute | solution.py:63
  266.5 13.6 %copy-start.18 = (bf16[128,1024]{1,0:T(8,128)(2,1)S(1)}, bf16[128,1024]{1,0:T(8,128)(2,1)}, u32[]{:S(2)}) copy-start(bf16[128,1024]{1,0:T(8,128)(2,1)} %copy-done.17) | copy-start | bytes 786436
  296.6 1.9 copy-start.5
  298.8 3.6 %copy-start.23 = (f32[1024]{0:T(1024)S(1)}, f32[1024]{0:T(1024)}, u32[]{:S(2)}) copy-start(f32[1024]{0:T(1024)} %param.26) | copy-start | bytes 12292
  307.5 1.0 copy-start.35
  308.5 2.6 copy-start.26
  308.5 2.6 copy-start.27
  308.6 2.6 copy-start.28
  308.6 2.6 copy-start.29
  308.6 2.6 copy-start.30
  308.6 2.6 copy-start.31
  308.6 2.6 copy-start.32
  314.6 35.3 %all-to-all-start.1 = ((bf16[8,128,128]{2,1,0:T(8,128)(2,1)}), bf16[8,128,128]{2,1,0:T(8,128)(2,1)}, u32[]{:S(2)}, u32[]{:S(2)}) async-start(bf16[8,128,128]{2,1,0:T(8,128)(2,1)} %bitcast.18), calls=%async_computation.1 | async-start | bytes 524288 | tf_op jit(solution)/shard_map/all_to_all | solution.py:69
  328.5 1.3 copy-start.7
  332.0 2.7 copy-start.10
  347.4 6.4 %copy-start.1 = (bf16[1024,1,384]{2,0,1:T(8,128)(2,1)S(1)}, bf16[1024,1,384]{2,0,1:T(8,128)(2,1)}, u32[]{:S(2)}) copy-start(bf16[1024,1,384]{2,0,1:T(8,128)(2,1)} %param.24) | copy-start | bytes 2359300
Sparse Core Ops, SparseCore 0:
  192.2 34.1 all-gather.5
  252.2 34.0 all-gather.7
  312.8 34.5 all-gather.9
